TPU v7x, 32 devices: a whole 2x2x4 slice. The times are simulated.
32 devices in a mesh: group: 2 (over y), site: 4 (over z), inner: 4 (over x, core).
Axes of the slice: x: 2, y: 2, z: 4, core: 2. Of those that a mesh axis runs over, the one named last changes fastest.
Arguments:
- activations: bfloat16 [8, 384, 2560], P(('group', 'site'), None, 'inner'), parts along dimension 0, may hold values from -6 to 6
- out_grads: bfloat16 [8, 384, 1024], P(('group', 'site')), parts along dimension 0, may hold values from -6 to 6
- site_weights: bfloat16 [8, 1024, 2560], P(('group', 'site'), None, 'inner'), parts along dimension 0, may hold values from -6 to 6
Outputs:
- merged: float32 [2048, 2560], P(('group', 'site'), 'inner'), parts along dimension 0
There are 2 independent parts, one for each index of `group`. A program takes and returns all parts, laid end to end along the dimension named above; each array names one. Nothing has to cross between parts.
All inputs are finite; a program needn't handle non-finite values.
Results may differ from a plain program's by a relative error of at most 0.0003.
Values sent between devices are 32-bit elements; how exact they have to be, the bound alone decides.
No kernel may reach another device: no remote copies, remote signals or barrier semaphores. Data moves between devices by JAX's collectives and lax.ppermute only.
A program may use at most 64 MiB of HBM per device.

v0:
```python
import jax
import jax.numpy as jnp
from jax import lax
from jax.sharding import PartitionSpec as P

ITERS = 4
damping = 1.0
highest = lax.Precision.HIGHEST


def local_term(columns, inputs, grads):
    count = inputs.shape[0]
    in_float = inputs.astype(jnp.float32)
    grad_float = grads.astype(jnp.float32)
    left_prod = jnp.dot(grad_float, columns, precision=highest)
    partial_value = jnp.dot(left_prod, in_float.T, precision=highest)
    token_pair = lax.psum(partial_value, "inner")
    mixed = (
        jnp.dot(token_pair, in_float, precision=highest) / (count * count)
        + damping * left_prod / count
    )
    return jnp.dot(grad_float.T, mixed, precision=highest)


def combine(term):
    return lax.psum_scatter(term, "site", scatter_dimension=0, tiled=True)


def spread(vector):
    return lax.all_gather(vector, "site", axis=0, tiled=True)


def apply_operator(vector, inputs, grads):
    return combine(local_term(spread(vector), inputs, grads))


def square_sum(residual):
    return lax.psum(jnp.sum(residual * residual), ("site", "inner"))


def per_device(activations, out_grads, site_weights):
    inputs = activations[0]
    grads = out_grads[0]
    rhs = combine(local_term(site_weights[0].astype(jnp.float32), inputs, grads))
    merged = jnp.zeros_like(rhs)
    residual = rhs
    direction = rhs
    norm_now = square_sum(residual)
    for count_step in range(ITERS):
        image = apply_operator(direction, inputs, grads)
        inner_prod = lax.psum(jnp.sum(direction * image), ("site", "inner"))
        alpha = norm_now / inner_prod
        merged = merged + alpha * direction
        residual = residual - alpha * image
        norm_next = square_sum(residual)
        direction = residual + norm_next / norm_now * direction
        norm_now = norm_next
    return merged


def solution(mesh):
    return jax.shard_map(
        per_device,
        mesh=mesh,
        in_specs=(
            P(("group", "site"), None, "inner"),
            P(("group", "site"), None, None),
            P(("group", "site"), None, "inner"),
        ),
        out_specs=P(("group", "site"), "inner"),
        check_vma=False,
    )
```

profile of v0, /device:TPU:0, one launch (start us, length us, event | category | flops | bytes accessed | tf_op | source)
XLA Modules:
  0.0 975.9 jit_solution(10916573341953800317)
XLA Ops:
  12.6 36.3 %all-reduce.7.cloned.1.call-done = f32[384,384]{1,0:T(8,128)} async-done(((f32[384,384]{1,0:T(8,128)}), f32[384,384]{1,0:T(8,128)}) %all-reduce.7.cloned.1.call-update) | async-done | bytes 589840 | tf_op jit(solution)/shard_map/psum | solution.py:17
  55.2 52.2 %reduce-scatter.6.cloned.1.call-done = f32[256,640]{0,1:T(8,128)} async-done(((f32[1024,640]{0,1:T(8,128)}), f32[256,640]{0,1:T(8,128)}) %reduce-scatter.6.cloned.1.call-update) | async-done | bytes 655376 | tf_op jit(solution)/shard_map/reduce_scatter | solution.py:26
  107.4 56.0 %all-gather.5.cloned.1.call-done = f32[1024,640]{0,1:T(8,128)} async-done(((f32[256,640]{0,1:T(8,128)}), f32[1024,640]{0,1:T(8,128)}) %all-gather.5.cloned.1.call-update) | async-done | bytes 2621456 | tf_op jit(solution)/shard_map/all_gather | solution.py:30
  163.4 3.9 fusion.17
  174.0 29.4 %all-reduce.9.cloned.1.call-done = f32[384,384]{1,0:T(8,128)} async-done(((f32[384,384]{1,0:T(8,128)}), f32[384,384]{1,0:T(8,128)}) %all-reduce.9.cloned.1.call-update) | async-done | bytes 589840 | tf_op jit(solution)/shard_map/psum | solution.py:17
  209.6 52.2 %reduce-scatter.8.cloned.1.call-done = f32[256,640]{0,1:T(8,128)} async-done(((f32[1024,640]{0,1:T(8,128)}), f32[256,640]{0,1:T(8,128)}) %reduce-scatter.8.cloned.1.call-update) | async-done | bytes 655376 | tf_op jit(solution)/shard_map/reduce_scatter | solution.py:26
  263.8 32.5 %all-reduce = (f32[]{:T(128)}, f32[]{:T(128)}) all-reduce(f32[]{:T(128)} %get-tuple-element.6, f32[]{:T(128)} %get-tuple-element.5), channel_id=1, replica_groups=mesh['group'=2,'site'=4,'inner'=4] {'site','inner'}, use_global_device_ids=true, to_apply=%region_3.0 | all-reduce | flops 2 | bytes 16 | tf_op jit(solution)/shard_map/psum | solution.py:38
  299.4 30.1 %psum.95 = f32[]{:T(128)} all-reduce(f32[]{:T(128)} %multiply_reduce_fusion.5), channel_id=1, replica_groups=mesh['group'=2,'site'=4,'inner'=4] {'site','inner'}, use_global_device_ids=true, to_apply=%region_9.0 | all-reduce | flops 1 | bytes 8 | tf_op jit(solution)/shard_map/psum | solution.py:38
  332.7 52.1 %all-gather.7.cloned.1.call-done = f32[1024,640]{0,1:T(8,128)} async-done(((f32[256,640]{0,1:T(8,128)}), f32[1024,640]{0,1:T(8,128)}) %all-gather.7.cloned.1.call-update) | async-done | bytes 2621456 | tf_op jit(solution)/shard_map/all_gather | solution.py:30
  384.8 3.9 fusion.14
  394.9 29.9 %all-reduce.11.cloned.1.call-done = f32[384,384]{1,0:T(8,128)} async-done(((f32[384,384]{1,0:T(8,128)}), f32[384,384]{1,0:T(8,128)}) %all-reduce.11.cloned.1.call-update) | async-done | bytes 589840 | tf_op jit(solution)/shard_map/psum | solution.py:17
  431.0 52.2 %reduce-scatter.10.cloned.1.call-done = f32[256,640]{0,1:T(8,128)} async-done(((f32[1024,640]{0,1:T(8,128)}), f32[256,640]{0,1:T(8,128)}) %reduce-scatter.10.cloned.1.call-update) | async-done | bytes 655376 | tf_op jit(solution)/shard_map/reduce_scatter | solution.py:26
  485.3 32.5 %psum.97 = f32[]{:T(128)} all-reduce(f32[]{:T(128)} %multiply_reduce_fusion.4), channel_id=1, replica_groups=mesh['group'=2,'site'=4,'inner'=4] {'site','inner'}, use_global_device_ids=true, to_apply=%region_13.0 | all-reduce | flops 1 | bytes 8 | tf_op jit(solution)/shard_map/psum | solution.py:51
  521.9 30.1 %psum.98 = f32[]{:T(128)} all-reduce(f32[]{:T(128)} %get-tuple-element.9), channel_id=1, replica_groups=mesh['group'=2,'site'=4,'inner'=4] {'site','inner'}, use_global_device_ids=true, to_apply=%region_15.0 | all-reduce | flops 1 | bytes 8 | tf_op jit(solution)/shard_map/psum | solution.py:38
  555.6 52.1 %all-gather.9.cloned.1.call-done = f32[1024,640]{0,1:T(8,128)} async-done(((f32[256,640]{0,1:T(8,128)}), f32[1024,640]{0,1:T(8,128)}) %all-gather.9.cloned.1.call-update) | async-done | bytes 2621456 | tf_op jit(solution)/shard_map/all_gather | solution.py:30
  607.7 3.9 fusion.11
  617.8 29.9 %all-reduce.13.cloned.1.call-done = f32[384,384]{1,0:T(8,128)} async-done(((f32[384,384]{1,0:T(8,128)}), f32[384,384]{1,0:T(8,128)}) %all-reduce.13.cloned.1.call-update) | async-done | bytes 589840 | tf_op jit(solution)/shard_map/psum | solution.py:17
  653.9 52.2 %reduce-scatter.12.cloned.1.call-done = f32[256,640]{0,1:T(8,128)} async-done(((f32[1024,640]{0,1:T(8,128)}), f32[256,640]{0,1:T(8,128)}) %reduce-scatter.12.cloned.1.call-update) | async-done | bytes 655376 | tf_op jit(solution)/shard_map/reduce_scatter | solution.py:26
  708.2 32.5 %psum.100 = f32[]{:T(128)} all-reduce(f32[]{:T(128)} %multiply_reduce_fusion.2), channel_id=1, replica_groups=mesh['group'=2,'site'=4,'inner'=4] {'site','inner'}, use_global_device_ids=true, to_apply=%region_19.0 | all-reduce | flops 1 | bytes 8 | tf_op jit(solution)/shard_map/psum | solution.py:51
  744.2 30.1 %psum.101 = f32[]{:T(128)} all-reduce(f32[]{:T(128)} %multiply_reduce_fusion.1), channel_id=1, replica_groups=mesh['group'=2,'site'=4,'inner'=4] {'site','inner'}, use_global_device_ids=true, to_apply=%region_21.0 | all-reduce | flops 1 | bytes 8 | tf_op jit(solution)/shard_map/psum | solution.py:38
  778.3 51.9 %all-gather.11.cloned.1.call-done = f32[1024,640]{0,1:T(8,128)} async-done(((f32[256,640]{0,1:T(8,128)}), f32[1024,640]{0,1:T(8,128)}) %all-gather.11.cloned.1.call-update) | async-done | bytes 2621456 | tf_op jit(solution)/shard_map/all_gather | solution.py:30
  840.3 29.9 %all-reduce.15.cloned.1.call-done = f32[384,384]{1,0:T(8,128)} async-done(((f32[384,384]{1,0:T(8,128)}), f32[384,384]{1,0:T(8,128)}) %all-reduce.15.cloned.1.call-update) | async-done | bytes 589840 | tf_op jit(solution)/shard_map/psum | solution.py:17
  876.4 52.3 %reduce-scatter.14.cloned.1.call-done = f32[256,640]{0,1:T(8,128)} async-done(((f32[1024,640]{0,1:T(8,128)}), f32[256,640]{0,1:T(8,128)}) %reduce-scatter.14.cloned.1.call-update) | async-done | bytes 655376 | tf_op jit(solution)/shard_map/reduce_scatter | solution.py:26
  930.8 32.6 %psum.103 = f32[]{:T(128)} all-reduce(f32[]{:T(128)} %multiply_reduce_fusion), channel_id=1, replica_groups=mesh['group'=2,'site'=4,'inner'=4] {'site','inner'}, use_global_device_ids=true, to_apply=%region_25.0 | all-reduce | flops 1 | bytes 8 | tf_op jit(solution)/shard_map/psum | solution.py:51
  (81 shorter events, 92.6 us)
Async XLA Ops:
  6.5 1.3 copy-start
  6.5 4.2 copy-start.2
  6.5 42.4 %all-reduce.7.cloned.1.call-start = ((), (), s32[]{:S(2)}) async-start(), calls=%async_computation.5 | async-start | bytes 1179648 | tf_op jit(solution)/shard_map/psum | solution.py:17
  9.8 1.0 copy-start.9
  10.7 40.6 %copy-start.1 = (bf16[1,384,1024]{2,1,0:T(8,128)(2,1)S(1)}, bf16[1,384,1024]{2,1,0:T(8,128)(2,1)}, u32[]{:S(2)}) copy-start(bf16[1,384,1024]{2,1,0:T(8,128)(2,1)} %param.4) | copy-start | bytes 2359300
  12.6 94.8 %reduce-scatter.6.cloned.1.call-start = ((), (), s32[]{:S(2)}) async-start(), calls=%async_computation.6 | async-start | bytes 3276800 | tf_op jit(solution)/shard_map/reduce_scatter | solution.py:26
  55.1 108.3 %all-gather.5.cloned.1.call-start = ((), (), s32[]{:S(2)}) async-start(), calls=%async_computation.7 | async-start | bytes 3276800 | tf_op jit(solution)/shard_map/all_gather | solution.py:30
  107.4 96.0 %all-reduce.9.cloned.1.call-start = ((), (), s32[]{:S(2)}) async-start(), calls=%async_computation.8 | async-start | bytes 1179648 | tf_op jit(solution)/shard_map/psum | solution.py:17
  167.4 1.0 copy-start.5
  170.9 90.9 %reduce-scatter.8.cloned.1.call-start = ((), (), s32[]{:S(2)}) async-start(), calls=%async_computation.9 | async-start | bytes 3276800 | tf_op jit(solution)/shard_map/reduce_scatter | solution.py:26
  205.8 56.0 %copy-start.3 = (f32[256,640]{0,1:T(8,128)S(1)}, f32[256,640]{0,1:T(8,128)}, u32[]{:S(2)}) copy-start(f32[256,640]{0,1:T(8,128)} %reduce-scatter.6.cloned.1.call-done) | copy-start | bytes 1966084
  209.6 175.3 %all-gather.7.cloned.1.call-start = ((), (), s32[]{:S(2)}) async-start(), calls=%async_computation.10 | async-start | bytes 3276800 | tf_op jit(solution)/shard_map/all_gather | solution.py:30
  332.7 92.1 %all-reduce.11.cloned.1.call-start = ((), (), s32[]{:S(2)}) async-start(), calls=%async_computation.11 | async-start | bytes 1179648 | tf_op jit(solution)/shard_map/psum | solution.py:17
  388.8 1.0 copy-start.6
  392.4 90.9 %reduce-scatter.10.cloned.1.call-start = ((), (), s32[]{:S(2)}) async-start(), calls=%async_computation.12 | async-start | bytes 3276800 | tf_op jit(solution)/shard_map/reduce_scatter | solution.py:26
  431.0 176.7 %all-gather.9.cloned.1.call-start = ((), (), s32[]{:S(2)}) async-start(), calls=%async_computation.13 | async-start | bytes 3276800 | tf_op jit(solution)/shard_map/all_gather | solution.py:30
  555.5 92.1 %all-reduce.13.cloned.1.call-start = ((), (), s32[]{:S(2)}) async-start(), calls=%async_computation.14 | async-start | bytes 1179648 | tf_op jit(solution)/shard_map/psum | solution.py:17
  611.6 1.0 copy-start.7
  615.2 90.9 %reduce-scatter.12.cloned.1.call-start = ((), (), s32[]{:S(2)}) async-start(), calls=%async_computation.15 | async-start | bytes 3276800 | tf_op jit(solution)/shard_map/reduce_scatter | solution.py:26
  653.8 176.4 %all-gather.11.cloned.1.call-start = ((), (), s32[]{:S(2)}) async-start(), calls=%async_computation.16 | async-start | bytes 3276800 | tf_op jit(solution)/shard_map/all_gather | solution.py:30
  778.1 92.1 %all-reduce.15.cloned.1.call-start = ((), (), s32[]{:S(2)}) async-start(), calls=%async_computation.17 | async-start | bytes 1179648 | tf_op jit(solution)/shard_map/psum | solution.py:17
  834.2 1.0 copy-start.8
  837.7 90.9 %reduce-scatter.14.cloned.1.call-start = ((), (), s32[]{:S(2)}) async-start(), calls=%async_computation.18 | async-start | bytes 3276800 | tf_op jit(solution)/shard_map/reduce_scatter | solution.py:26
  876.3 88.4 %copy-start.4 = (f32[256,640]{0,1:T(8,128)S(1)}, f32[256,640]{0,1:T(8,128)}, u32[]{:S(2)}) copy-start(f32[256,640]{0,1:T(8,128)} %multiply_add_fusion.3) | copy-start | bytes 1966084
Sparse Core Ops, SparseCore 0:
  12.7 36.1 all-reduce.6
  55.2 52.0 reduce-scatter.5
  108.9 54.4 all-gather.4
  171.1 32.2 all-reduce.8
  209.7 52.0 reduce-scatter.7
  332.8 51.9 all-gather.6
  392.5 32.2 all-reduce.10
  431.1 52.0 reduce-scatter.9
  555.7 51.9 all-gather.8
  615.3 32.2 all-reduce.12
  653.9 52.0 reduce-scatter.11
  778.2 51.9 all-gather.10
  837.9 32.2 all-reduce.14
  876.5 52.0 reduce-scatter.13
where the time goes:
time: 984 us; the launch traced here: 976 us
  waiting for transfers between devices  629 us (64%)
  blocking collectives  220 us (22%)
  matrix products  60.5 us (6%)
  other arithmetic  24.1 us (2%)
  between operations  22.5 us (2%)
  local copies, waits for them, and re-layouts  18.3 us (2%)
    reduce_scatter x5, waiting for transfers between devices, combine(): return lax.psum_scatter(term, 'site', scatter_dimension=0, tiled=True)  261 us
    all_gather x4, waiting for transfers between devices, spread(): return lax.all_gather(vector, 'site', axis=0, tiled=True)  212 us
    psum x5, waiting for transfers between devices, local_term(): token_pair = lax.psum(partial_value, 'inner')  155 us
    psum x4, blocking collectives, square_sum(): return lax.psum(jnp.sum(residual * residual), ('site', 'inner'))  123 us
    psum x3, blocking collectives, per_device(): inner_prod = lax.psum(jnp.sum(direction * image), ('site', 'inner'))  97.6 us
  transfers between devices with their start and end apart: 14, of which 14 were waited for; matrix products, arithmetic and copies ran while one was open for 1% of the time, Pallas kernels for 0%

commit v1 on v0

--- a/solution.py
+++ b/solution.py
@@ -6,6 +6,28 @@
 ITERS = 4
 damping = 1.0
 highest = lax.Precision.HIGHEST
+
+
+def joined_along(blocks, dim):
+    shape = list(blocks.shape[1:])
+    shape[dim] *= blocks.shape[0]
+    return jnp.moveaxis(blocks, 0, dim).reshape(shape)
+
+
+def doubled(x, axis):
+    devices = lax.axis_size(axis)
+    pieces = x[None]
+    for level in range(devices.bit_length() - 1):
+        distance = 1 << level
+        other = lax.ppermute(pieces, axis, [(i, i ^ distance) for i in range(devices)])
+        both = jnp.stack([pieces, other])
+        upper = lax.axis_index(axis) >> level & 1
+        pieces = jnp.where(upper == 0, both, both[::-1]).reshape(-1, *x.shape)
+    return pieces
+
+
+def gather_by_bits(x, axis, dim):
+    return joined_along(doubled(x, axis), dim)
 
 
 def local_term(columns, inputs, grads):
@@ -27,7 +49,7 @@
 
 
 def spread(vector):
-    return lax.all_gather(vector, "site", axis=0, tiled=True)
+    return gather_by_bits(vector, "site", 0)
 
 
 def apply_operator(vector, inputs, grads):

time: 984 us -> 1100 us (1.12)
  waiting for transfers between devices: 629 us -> 713 us
    ppermute x0 -> x8, waiting for transfers between devices: none -> 298 us  [doubled(): lax.ppermute(pieces, axis, [(i, i ^ distance) for i in range(devices)])]
    all_gather x4 -> x0, waiting for transfers between devices: 212 us -> none  [spread(): return lax.all_gather(vector, 'site', axis=0, tiled=True)]
    select_n x0 -> x4, local copies, waits for them, and re-layouts: none -> 13 us  [doubled(): pieces = jnp.where(upper == 0, both, both[::-1]).reshape(-1, *x.shape)]
  transfers between devices with their start and end apart: 14 -> 18, of which waited for: 14 -> 18; matrix products, arithmetic and copies ran while one was open for 1% -> 1% of each run, Pallas kernels for 0% -> 0%
where the time goes in v1:
time: 1100 us; the launch traced here: 1090 us
  waiting for transfers between devices  713 us (65%)
  blocking collectives  221 us (20%)
  matrix products  68.3 us (6%)
  other arithmetic  33.5 us (3%)
  local copies, waits for them, and re-layouts  28.2 us (3%)
  between operations  23.1 us (2%)
    ppermute x8, waiting for transfers between devices, doubled(): lax.ppermute(pieces, axis, [(i, i ^ distance) for i in range(devices)])  298 us
    reduce_scatter x5, waiting for transfers between devices, combine(): return lax.psum_scatter(term, 'site', scatter_dimension=0, tiled=True)  261 us
    psum x5, waiting for transfers between devices, local_term(): token_pair = lax.psum(partial_value, 'inner')  154 us
    psum x4, blocking collectives, square_sum(): return lax.psum(jnp.sum(residual * residual), ('site', 'inner'))  124 us
    psum x3, blocking collectives, per_device(): inner_prod = lax.psum(jnp.sum(direction * image), ('site', 'inner'))  97.5 us
    dot_general x5, matrix products, local_term(): left_prod = jnp.dot(grad_float, columns, precision=highest)  25.8 us
  transfers between devices with their start and end apart: 18, of which 18 were waited for; matrix products, arithmetic and copies ran while one was open for 1% of the time, Pallas kernels for 0%

profile of v1, /device:TPU:0, one launch (start us, length us, event | category | flops | bytes accessed | tf_op | source)
XLA Modules:
  0.0 1091.0 jit_solution(9450164895850662734)
XLA Ops:
  11.7 36.2 %all-reduce.7.cloned.1.call-done = f32[384,384]{1,0:T(8,128)} async-done(((f32[384,384]{1,0:T(8,128)}), f32[384,384]{1,0:T(8,128)}) %all-reduce.7.cloned.1.call-update) | async-done | bytes 589840 | tf_op jit(solution)/shard_map/psum | solution.py:39
  54.0 52.0 %reduce-scatter.6.cloned.1.call-done = f32[256,640]{0,1:T(8,128)} async-done(((f32[1024,640]{0,1:T(8,128)}), f32[256,640]{0,1:T(8,128)}) %reduce-scatter.6.cloned.1.call-update) | async-done | bytes 655376 | tf_op jit(solution)/shard_map/reduce_scatter | solution.py:48
  127.3 56.4 %collective-permute-done.1 = f32[2,256,640]{1,2,0:T(8,128)} collective-permute-done((f32[2,256,640]{1,2,0:T(8,128)}, f32[2,256,640]{1,2,0:T(8,128)}, u32[]{:S(2)}, u32[]{:S(2)}) %collective-permute-start.1) | collective-permute-done | bytes 1310752 | tf_op jit(solution)/shard_map/ppermute | solution.py:22
  200.2 32.3 %all-reduce.9.cloned.1.call-done = f32[384,384]{1,0:T(8,128)} async-done(((f32[384,384]{1,0:T(8,128)}), f32[384,384]{1,0:T(8,128)}) %all-reduce.9.cloned.1.call-update) | async-done | bytes 589840 | tf_op jit(solution)/shard_map/psum | solution.py:39
  238.7 52.2 %reduce-scatter.8.cloned.1.call-done = f32[256,640]{0,1:T(8,128)} async-done(((f32[1024,640]{0,1:T(8,128)}), f32[256,640]{0,1:T(8,128)}) %reduce-scatter.8.cloned.1.call-update) | async-done | bytes 655376 | tf_op jit(solution)/shard_map/reduce_scatter | solution.py:48
  292.9 32.6 %all-reduce = (f32[]{:T(128)}, f32[]{:T(128)}) all-reduce(f32[]{:T(128)} %get-tuple-element.6, f32[]{:T(128)} %get-tuple-element.5), channel_id=1, replica_groups=mesh['group'=2,'site'=4,'inner'=4] {'site','inner'}, use_global_device_ids=true, to_apply=%region_3.0 | all-reduce | flops 2 | bytes 16 | tf_op jit(solution)/shard_map/psum | solution.py:60
  328.7 30.3 %psum.95 = f32[]{:T(128)} all-reduce(f32[]{:T(128)} %multiply_reduce_fusion.5), channel_id=1, replica_groups=mesh['group'=2,'site'=4,'inner'=4] {'site','inner'}, use_global_device_ids=true, to_apply=%region_9.10 | all-reduce | flops 1 | bytes 8 | tf_op jit(solution)/shard_map/psum | solution.py:60
  361.6 16.5 %collective-permute-done.2 = f32[1,256,640]{1,2,0:T(8,128)S(1)} collective-permute-done((f32[1,256,640]{1,2,0:T(8,128)S(1)}, f32[1,256,640]{1,2,0:T(8,128)S(1)}, u32[]{:S(2)}, u32[]{:S(2)}) %collective-permute-start.2) | collective-permute-done | bytes 655392 | tf_op jit(solution)/shard_map/ppermute | solution.py:22
  378.4 58.7 %collective-permute-done.3 = f32[2,256,640]{1,2,0:T(8,128)S(1)} collective-permute-done((f32[2,256,640]{1,2,0:T(8,128)S(1)}, f32[2,256,640]{1,2,0:T(8,128)S(1)}, u32[]{:S(2)}, u32[]{:S(2)}) %collective-permute-start.3) | collective-permute-done | bytes 1310752 | tf_op jit(solution)/shard_map/ppermute | solution.py:22
  454.4 28.5 %all-reduce.11.cloned.1.call-done = f32[384,384]{1,0:T(8,128)} async-done(((f32[384,384]{1,0:T(8,128)}), f32[384,384]{1,0:T(8,128)}) %all-reduce.11.cloned.1.call-update) | async-done | bytes 589840 | tf_op jit(solution)/shard_map/psum | solution.py:39
  489.1 52.2 %reduce-scatter.10.cloned.1.call-done = f32[256,640]{0,1:T(8,128)} async-done(((f32[1024,640]{0,1:T(8,128)}), f32[256,640]{0,1:T(8,128)}) %reduce-scatter.10.cloned.1.call-update) | async-done | bytes 655376 | tf_op jit(solution)/shard_map/reduce_scatter | solution.py:48
  543.2 32.5 %psum.97 = f32[]{:T(128)} all-reduce(f32[]{:T(128)} %multiply_reduce_fusion.4), channel_id=1, replica_groups=mesh['group'=2,'site'=4,'inner'=4] {'site','inner'}, use_global_device_ids=true, to_apply=%region_13.14 | all-reduce | flops 1 | bytes 8 | tf_op jit(solution)/shard_map/psum | solution.py:73
  579.8 30.6 %psum.98 = f32[]{:T(128)} all-reduce(f32[]{:T(128)} %get-tuple-element.9), channel_id=1, replica_groups=mesh['group'=2,'site'=4,'inner'=4] {'site','inner'}, use_global_device_ids=true, to_apply=%region_15.16 | all-reduce | flops 1 | bytes 8 | tf_op jit(solution)/shard_map/psum | solution.py:60
  612.9 16.5 %collective-permute-done.4 = f32[1,256,640]{1,2,0:T(8,128)S(1)} collective-permute-done((f32[1,256,640]{1,2,0:T(8,128)S(1)}, f32[1,256,640]{1,2,0:T(8,128)S(1)}, u32[]{:S(2)}, u32[]{:S(2)}) %collective-permute-start.4) | collective-permute-done | bytes 655392 | tf_op jit(solution)/shard_map/ppermute | solution.py:22
  629.8 58.7 %collective-permute-done.5 = f32[2,256,640]{1,2,0:T(8,128)S(1)} collective-permute-done((f32[2,256,640]{1,2,0:T(8,128)S(1)}, f32[2,256,640]{1,2,0:T(8,128)S(1)}, u32[]{:S(2)}, u32[]{:S(2)}) %collective-permute-start.5) | collective-permute-done | bytes 1310752 | tf_op jit(solution)/shard_map/ppermute | solution.py:22
  705.8 28.5 %all-reduce.13.cloned.1.call-done = f32[384,384]{1,0:T(8,128)} async-done(((f32[384,384]{1,0:T(8,128)}), f32[384,384]{1,0:T(8,128)}) %all-reduce.13.cloned.1.call-update) | async-done | bytes 589840 | tf_op jit(solution)/shard_map/psum | solution.py:39
  740.5 52.2 %reduce-scatter.12.cloned.1.call-done = f32[256,640]{0,1:T(8,128)} async-done(((f32[1024,640]{0,1:T(8,128)}), f32[256,640]{0,1:T(8,128)}) %reduce-scatter.12.cloned.1.call-update) | async-done | bytes 655376 | tf_op jit(solution)/shard_map/reduce_scatter | solution.py:48
  794.8 32.5 %psum.100 = f32[]{:T(128)} all-reduce(f32[]{:T(128)} %multiply_reduce_fusion.2), channel_id=1, replica_groups=mesh['group'=2,'site'=4,'inner'=4] {'site','inner'}, use_global_device_ids=true, to_apply=%region_19.20 | all-reduce | flops 1 | bytes 8 | tf_op jit(solution)/shard_map/psum | solution.py:73
  830.6 30.3 %psum.101 = f32[]{:T(128)} all-reduce(f32[]{:T(128)} %multiply_reduce_fusion.1), channel_id=1, replica_groups=mesh['group'=2,'site'=4,'inner'=4] {'site','inner'}, use_global_device_ids=true, to_apply=%region_21.22 | all-reduce | flops 1 | bytes 8 | tf_op jit(solution)/shard_map/psum | solution.py:60
  863.9 16.5 %collective-permute-done.6 = f32[1,256,640]{1,2,0:T(8,128)S(1)} collective-permute-done((f32[1,256,640]{1,2,0:T(8,128)S(1)}, f32[1,256,640]{1,2,0:T(8,128)S(1)}, u32[]{:S(2)}, u32[]{:S(2)}) %collective-permute-start.6) | collective-permute-done | bytes 655392 | tf_op jit(solution)/shard_map/ppermute | solution.py:22
  880.8 58.7 %collective-permute-done.7 = f32[2,256,640]{1,2,0:T(8,128)S(1)} collective-permute-done((f32[2,256,640]{1,2,0:T(8,128)S(1)}, f32[2,256,640]{1,2,0:T(8,128)S(1)}, u32[]{:S(2)}, u32[]{:S(2)}) %collective-permute-start.7) | collective-permute-done | bytes 1310752 | tf_op jit(solution)/shard_map/ppermute | solution.py:22
  956.8 28.5 %all-reduce.15.cloned.1.call-done = f32[384,384]{1,0:T(8,128)} async-done(((f32[384,384]{1,0:T(8,128)}), f32[384,384]{1,0:T(8,128)}) %all-reduce.15.cloned.1.call-update) | async-done | bytes 589840 | tf_op jit(solution)/shard_map/psum | solution.py:39
  991.4 52.3 %reduce-scatter.14.cloned.1.call-done = f32[256,640]{0,1:T(8,128)} async-done(((f32[1024,640]{0,1:T(8,128)}), f32[256,640]{0,1:T(8,128)}) %reduce-scatter.14.cloned.1.call-update) | async-done | bytes 655376 | tf_op jit(solution)/shard_map/reduce_scatter | solution.py:48
  1045.8 32.5 %psum.103 = f32[]{:T(128)} all-reduce(f32[]{:T(128)} %multiply_reduce_fusion), channel_id=1, replica_groups=mesh['group'=2,'site'=4,'inner'=4] {'site','inner'}, use_global_device_ids=true, to_apply=%region_25.26 | all-reduce | flops 1 | bytes 8 | tf_op jit(solution)/shard_map/psum | solution.py:73
  (105 shorter events, 150.0 us)
Async XLA Ops:
  6.5 3.2 copy-start.3
  6.5 41.4 %all-reduce.7.cloned.1.call-start = ((), (), s32[]{:S(2)}) async-start(), calls=%async_computation.5 | async-start | bytes 1179648 | tf_op jit(solution)/shard_map/psum | solution.py:39
  9.8 40.2 %copy-start.2 = (bf16[1,384,1024]{2,1,0:T(8,128)(2,1)S(1)}, bf16[1,384,1024]{2,1,0:T(8,128)(2,1)}, u32[]{:S(2)}) copy-start(bf16[1,384,1024]{2,1,0:T(8,128)(2,1)} %param.4) | copy-start | bytes 2359300
  11.6 94.4 %reduce-scatter.6.cloned.1.call-start = ((), (), s32[]{:S(2)}) async-start(), calls=%async_computation.6 | async-start | bytes 3276800 | tf_op jit(solution)/shard_map/reduce_scatter | solution.py:48
  53.8 178.7 %all-reduce.9.cloned.1.call-start = ((), (), s32[]{:S(2)}) async-start(), calls=%async_computation.7 | async-start | bytes 1179648 | tf_op jit(solution)/shard_map/psum | solution.py:39
  106.1 16.5 %collective-permute-start = (f32[1,256,640]{1,2,0:T(8,128)}, f32[1,256,640]{1,2,0:T(8,128)S(1)}, u32[]{:S(2)}, u32[]{:S(2)}) collective-permute-start(f32[1,256,640]{1,2,0:T(8,128)} %bitcast.124), channel_id=1, source_target_pairs={{0,4},{4,0},{8,12},{12,8},{1,5},{5,1},{9,13},{13,9},{2,6},{6,2},{1... | collective-permute-start | bytes 1966088 | tf_op jit(solution)/shard_map/ppermute | solution.py:22
  125.0 58.8 %collective-permute-start.1 = (f32[2,256,640]{1,2,0:T(8,128)}, f32[2,256,640]{1,2,0:T(8,128)}, u32[]{:S(2)}, u32[]{:S(2)}) collective-permute-start(f32[2,256,640]{1,2,0:T(8,128)} %get-tuple-element.18), channel_id=1, source_target_pairs={{0,8},{4,12},{8,0},{12,4},{1,9},{5,13},{9,1},{13,5},{2,10},{6,14},... | collective-permute-start | bytes 3932168 | tf_op jit(solution)/shard_map/ppermute | solution.py:22
  198.8 92.1 %reduce-scatter.8.cloned.1.call-start = ((), (), s32[]{:S(2)}) async-start(), calls=%async_computation.8 | async-start | bytes 3276800 | tf_op jit(solution)/shard_map/reduce_scatter | solution.py:48
  234.9 56.0 %copy-start.4 = (f32[256,640]{0,1:T(8,128)S(1)}, f32[256,640]{0,1:T(8,128)}, u32[]{:S(2)}) copy-start(f32[256,640]{0,1:T(8,128)} %reduce-scatter.6.cloned.1.call-done) | copy-start | bytes 1966084
  238.7 244.2 %all-reduce.11.cloned.1.call-start = ((), (), s32[]{:S(2)}) async-start(), calls=%async_computation.9 | async-start | bytes 1179648 | tf_op jit(solution)/shard_map/psum | solution.py:39
  361.5 16.6 %collective-permute-start.2 = (f32[1,256,640]{1,2,0:T(8,128)S(1)}, f32[1,256,640]{1,2,0:T(8,128)S(1)}, u32[]{:S(2)}, u32[]{:S(2)}) collective-permute-start(f32[1,256,640]{1,2,0:T(8,128)S(1)} %bitcast.126), channel_id=1, source_target_pairs={{0,4},{4,0},{8,12},{12,8},{1,5},{5,1},{9,13},{13,9},{2,6},{6,2},{1... | collective-permute-start | bytes 1966088 | tf_op jit(solution)/shard_map/ppermute | solution.py:22
  378.3 58.7 %collective-permute-start.3 = (f32[2,256,640]{1,2,0:T(8,128)S(1)}, f32[2,256,640]{1,2,0:T(8,128)S(1)}, u32[]{:S(2)}, u32[]{:S(2)}) collective-permute-start(f32[2,256,640]{1,2,0:T(8,128)S(1)} %get-tuple-element.16), channel_id=1, source_target_pairs={{0,8},{4,12},{8,0},{12,4},{1,9},{5,13},{9,1},{13,5},{2,10},{6,14},... | collective-permute-start | bytes 3932168 | tf_op jit(solution)/shard_map/ppermute | solution.py:22
  451.8 89.5 %reduce-scatter.10.cloned.1.call-start = ((), (), s32[]{:S(2)}) async-start(), calls=%async_computation.10 | async-start | bytes 3276800 | tf_op jit(solution)/shard_map/reduce_scatter | solution.py:48
  489.0 245.2 %all-reduce.13.cloned.1.call-start = ((), (), s32[]{:S(2)}) async-start(), calls=%async_computation.11 | async-start | bytes 1179648 | tf_op jit(solution)/shard_map/psum | solution.py:39
  612.8 16.6 %copy-start.5 = (f32[256,640]{0,1:T(8,128)}, f32[256,640]{0,1:T(8,128)S(1)}, u32[]{:S(2)}) copy-start(f32[256,640]{0,1:T(8,128)S(1)} %multiply_add_fusion.2) | copy-start | bytes 1966084
  612.8 16.6 %collective-permute-start.4 = (f32[1,256,640]{1,2,0:T(8,128)S(1)}, f32[1,256,640]{1,2,0:T(8,128)S(1)}, u32[]{:S(2)}, u32[]{:S(2)}) collective-permute-start(f32[1,256,640]{1,2,0:T(8,128)S(1)} %bitcast.128), channel_id=1, source_target_pairs={{0,4},{4,0},{8,12},{12,8},{1,5},{5,1},{9,13},{13,9},{2,6},{6,2},{1... | collective-permute-start | bytes 1966088 | tf_op jit(solution)/shard_map/ppermute | solution.py:22
  629.7 58.7 %collective-permute-start.5 = (f32[2,256,640]{1,2,0:T(8,128)S(1)}, f32[2,256,640]{1,2,0:T(8,128)S(1)}, u32[]{:S(2)}, u32[]{:S(2)}) collective-permute-start(f32[2,256,640]{1,2,0:T(8,128)S(1)} %get-tuple-element.14), channel_id=1, source_target_pairs={{0,8},{4,12},{8,0},{12,4},{1,9},{5,13},{9,1},{13,5},{2,10},{6,14},... | collective-permute-start | bytes 3932168 | tf_op jit(solution)/shard_map/ppermute | solution.py:22
  703.2 89.5 %reduce-scatter.12.cloned.1.call-start = ((), (), s32[]{:S(2)}) async-start(), calls=%async_computation.12 | async-start | bytes 3276800 | tf_op jit(solution)/shard_map/reduce_scatter | solution.py:48
  740.4 244.8 %all-reduce.15.cloned.1.call-start = ((), (), s32[]{:S(2)}) async-start(), calls=%async_computation.13 | async-start | bytes 1179648 | tf_op jit(solution)/shard_map/psum | solution.py:39
  863.8 16.6 %copy-start.6 = (f32[256,640]{0,1:T(8,128)}, f32[256,640]{0,1:T(8,128)S(1)}, u32[]{:S(2)}) copy-start(f32[256,640]{0,1:T(8,128)S(1)} %multiply_add_fusion.1) | copy-start | bytes 1966084
  863.8 16.6 %collective-permute-start.6 = (f32[1,256,640]{1,2,0:T(8,128)S(1)}, f32[1,256,640]{1,2,0:T(8,128)S(1)}, u32[]{:S(2)}, u32[]{:S(2)}) collective-permute-start(f32[1,256,640]{1,2,0:T(8,128)S(1)} %bitcast.134), channel_id=1, source_target_pairs={{0,4},{4,0},{8,12},{12,8},{1,5},{5,1},{9,13},{13,9},{2,6},{6,2},{1... | collective-permute-start | bytes 1966088 | tf_op jit(solution)/shard_map/ppermute | solution.py:22
  880.7 58.7 %collective-permute-start.7 = (f32[2,256,640]{1,2,0:T(8,128)S(1)}, f32[2,256,640]{1,2,0:T(8,128)S(1)}, u32[]{:S(2)}, u32[]{:S(2)}) collective-permute-start(f32[2,256,640]{1,2,0:T(8,128)S(1)} %get-tuple-element.12), channel_id=1, source_target_pairs={{0,8},{4,12},{8,0},{12,4},{1,9},{5,13},{9,1},{13,5},{2,10},{6,14},... | collective-permute-start | bytes 3932168 | tf_op jit(solution)/shard_map/ppermute | solution.py:22
  954.2 89.5 %reduce-scatter.14.cloned.1.call-start = ((), (), s32[]{:S(2)}) async-start(), calls=%async_computation.14 | async-start | bytes 3276800 | tf_op jit(solution)/shard_map/reduce_scatter | solution.py:48
  1043.7 40.3 %copy-start.1 = (bf16[1,1024,640]{2,1,0:T(8,128)(2,1)S(1)}, bf16[1,1024,640]{2,1,0:T(8,128)(2,1)}, u32[]{:S(2)}) copy-start(bf16[1,1024,640]{2,1,0:T(8,128)(2,1)} %param.5) | copy-start | bytes 3932164
  (4 other events, 4.2 us)
Sparse Core Ops, SparseCore 0:
  11.8 36.1 all-reduce.6
  53.9 52.0 reduce-scatter.5
  199.0 33.4 all-reduce.8
  238.8 52.0 reduce-scatter.7
  451.9 30.8 all-reduce.10
  489.2 52.0 reduce-scatter.9
  703.3 30.8 all-reduce.12
  740.6 52.0 reduce-scatter.11
  954.3 30.8 all-reduce.14
  991.5 52.0 reduce-scatter.13
